TPU v7x, 512 devices: a whole 4x4x16 slice. The times are simulated.
512 devices in a mesh: expert: 8 (over y, core), mp: 64 (over x, z).
Axes of the slice: x: 4, y: 4, z: 16, core: 2. Of those that a mesh axis runs over, the one named last changes fastest.
Arguments:
- context: bfloat16 [4096, 2048], P('expert', 'mp'), may hold values from -6 to 6
- out_proj: bfloat16 [2048, 2048], P('mp'), may hold values from -1 to 1, as said below
- routes: int32 [4096, 2], P('expert'), may hold values from 0 to 7, all different within a row; in each aligned block of 512 rows (0 to 511, 512 to 1023, ...) at most 256 rows name the same one
- router_logits: float32 [4096, 2], P('expert'), may hold values from -8 to 8
- w_gate: bfloat16 [45056, 2048], P('mp', 'expert'), may hold values from -0.125 to 0.125
- w_up: bfloat16 [45056, 2048], P('mp', 'expert'), may hold values from -0.125 to 0.125
- w_down: bfloat16 [45056, 2048], P('mp', 'expert'), may hold values from -0.078125 to 0.078125
- norm_gain: float32 [2048], P('mp'), may hold values from 0.25 to 1.75
- request_order: int32 [4096], P('expert'), may hold values from 0 to 4095, each once
Outputs:
- restored: bfloat16 [4096, 2048], P('expert', 'mp')
Inputs may be any that keep to these rules, and one draw needn't show every extreme that they name: `routes`: each row names 2 different experts. Within each aligned block of 512 rows no expert is named by more than 256 rows, and in some blocks one expert is named by exactly 256 rows. `request_order`: A permutation of the 4096 token rows. `out_proj`: entries of the order of one over the square root of 2048.
All inputs are finite; a program needn't handle non-finite values.
Results may differ from a plain program's by a relative error of at most 0.0056.
Values may be sent and summed in bfloat16 or wider, within the bound.
No kernel may reach another device: no remote copies, remote signals or barrier semaphores. Data moves between devices by JAX's collectives and lax.ppermute only.
A program may use at most 64 MiB of HBM per device.

v0:
```python
import jax
import jax.numpy as jnp
from jax import lax
from jax.sharding import Mesh, PartitionSpec as P

EXPERTS = 8
CAP = 256
epsilon = 1e-06


def slot_targets(routes, capacity, experts):
    flat_routes = routes.reshape(-1)
    onehot = (flat_routes[:, None] == jnp.arange(experts, dtype=jnp.int32)[None, :]).astype(
        jnp.int32
    )
    earlier = jnp.cumsum(onehot, axis=0) - onehot
    slot_index = jnp.sum(earlier * onehot, axis=1)
    return flat_routes * capacity + slot_index


def shards(
    context, out_proj, routes, router_logits, w_gate, w_up, w_down, norm_gain, request_order
):
    tok_rows = context.shape[0]
    feat_local = context.shape[1]
    model_width = out_proj.shape[1]
    mp_count = lax.axis_size(MP)
    copies = mp_count // EXPERTS
    capacity = CAP
    top_k = routes.shape[1]
    x_count = lax.axis_size("mx")
    x_at = lax.axis_index("mx")
    along_z = lax.all_gather(context, MZ, axis=1, tiled=True)
    z_width = along_z.shape[1]
    rows_x = lax.all_to_all(
        jnp.broadcast_to(out_proj[None], (x_count,) + out_proj.shape),
        "mx",
        split_axis=0,
        concat_axis=0,
        tiled=True,
    ).reshape(x_count * feat_local, model_width)
    rows_x = lax.dynamic_slice_in_dim(rows_x, x_at * z_width, z_width, axis=1)
    partial_attended = jnp.einsum("td,cd->tc", along_z, rows_x, preferred_element_type=jnp.float32)
    attended = jnp.sum(
        lax.all_to_all(
            partial_attended.reshape(tok_rows, x_count, feat_local),
            "mx",
            split_axis=1,
            concat_axis=1,
            tiled=True,
        ),
        axis=1,
    ).astype(jnp.bfloat16)
    destination = slot_targets(routes, capacity, EXPERTS)
    source_rows = jnp.repeat(jnp.arange(tok_rows, dtype=jnp.int32), top_k)
    slotted = (
        jnp.zeros((EXPERTS * capacity, feat_local), jnp.bfloat16)
        .at[destination]
        .set(attended[source_rows])
    )
    one_copy = lax.all_to_all(
        slotted.reshape(EXPERTS, capacity, feat_local),
        ("mx", "mzh"),
        split_axis=0,
        concat_axis=0,
        tiled=True,
    )
    inbox_rows = (
        lax.all_gather(one_copy, "mzl", axis=0)
        .transpose(2, 1, 0, 3)
        .reshape(capacity, mp_count * feat_local)
    )
    stacked = lax.all_gather(jnp.stack([w_gate, w_up, w_down]), EX, axis=2, tiled=True)
    gate_next = jnp.einsum("rd,hd->rh", inbox_rows, stacked[0], preferred_element_type=jnp.float32)
    up_next = jnp.einsum("rd,hd->rh", inbox_rows, stacked[1], preferred_element_type=jnp.float32)
    activated = (jax.nn.silu(gate_next) * up_next).astype(jnp.bfloat16)
    partial_value = jnp.dot(activated, stacked[2], preferred_element_type=jnp.float32)
    returned = lax.all_to_all(
        partial_value.astype(jnp.bfloat16), MP, split_axis=1, concat_axis=0, tiled=True
    )
    expert_out = jnp.sum(
        returned.reshape(EXPERTS, copies, capacity, feat_local).astype(jnp.float32), axis=1
    ).reshape(EXPERTS * capacity, feat_local)
    picked = expert_out[destination].reshape(tok_rows, top_k, feat_local)
    weights = 1.0 / (1.0 + jnp.exp(router_logits[:, ::-1] - router_logits))
    branch = jnp.sum(picked * weights[:, :, None], axis=1)
    combined = attended.astype(jnp.float32) + branch
    squares = jnp.sum(lax.all_gather(jnp.sum(combined * combined, axis=1), MZ, axis=0), axis=0)
    squares = jnp.sum(lax.all_gather(squares, "mx", axis=0), axis=0)
    normed = (
        combined * norm_gain[None, :] * lax.rsqrt(squares / model_width + epsilon)[:, None]
    ).astype(jnp.bfloat16)
    everyone = lax.all_gather(normed, EX, axis=0, tiled=True)
    return everyone[request_order]


EX = ("ey", "ec")
MZ = ("mzh", "mzl")
MP = ("mx",) + MZ


def split_mesh(mesh):
    devices = mesh.devices
    n_exp, n_mp = devices.shape
    row = devices[0].reshape(-1)
    try:
        z_count = len({d.coords[2] for d in row})
    except (AttributeError, IndexError, TypeError):
        z_count = n_mp
    group = n_mp // EXPERTS
    return Mesh(
        devices.reshape(1, n_exp, n_mp // z_count, z_count // group, group),
        ("ey", "ec", "mx", "mzh", "mzl"),
    )


def solution(mesh):
    fine = split_mesh(mesh)
    placed = (
        P(EX, MP),
        P(MP, None),
        P(EX, None),
        P(EX, None),
        P(MP, EX),
        P(MP, EX),
        P(MP, EX),
        P(MP),
        P(EX),
    )
    return jax.shard_map(shards, mesh=fine, in_specs=placed, out_specs=P(EX, MP), check_vma=False)
```

profile of v0, /device:TPU:1, one launch (start us, length us, event | category | flops | bytes accessed | tf_op | source)
XLA Modules:
  0.0 365.1 jit_solution(336323215488150138)
XLA Ops:
  6.5 1.7 broadcast_in_dim.8
  8.3 4.8 %all-to-all-start = ((bf16[4,32,2048]{2,1,0:T(8,128)(2,1)}), bf16[4,32,2048]{2,1,0:T(8,128)(2,1)S(1)}, u32[]{:S(2)}, u32[]{:S(2)}) async-start(bf16[4,32,2048]{2,1,0:T(8,128)(2,1)} %broadcast_in_dim.8), calls=%async_computation | async-start | bytes 1048576 | tf_op jit(solution)/shard_map/all_to_all | solution.py:35
  15.1 2.3 reduce-window.6
  18.5 31.9 %all_gather.27 = bf16[512,512]{0,1:T(8,128)(2,1)S(1)} all-gather(bf16[512,32]{0,1:T(8,128)(2,1)S(1)} %copy-done.3), channel_id=1, replica_groups=mesh['ey'=1,'ec'=8,'mx'=4,'mzh'=2,'mzl'=8] {'mzh','mzl'}, dimensions={1}, use_global_device_ids=true | all-gather | bytes 557056 | tf_op jit(solution)/shard_map/all_gather | solution.py:33
  50.5 0.9 fusion.15
  51.4 4.1 %all-to-all-start.1 = ((f32[512,4,32]{0,2,1:T(8,128)}), f32[512,4,32]{0,2,1:T(8,128)S(1)}, u32[]{:S(2)}, u32[]{:S(2)}) async-start(f32[512,4,32]{0,2,1:T(8,128)} %bitcast.2), calls=%async_computation.1 | async-start | bytes 524288 | tf_op jit(solution)/shard_map/all_to_all | solution.py:45
  55.5 5.5 %all-to-all-done.1 = f32[512,4,32]{0,2,1:T(8,128)S(1)} async-done(((f32[512,4,32]{0,2,1:T(8,128)}), f32[512,4,32]{0,2,1:T(8,128)S(1)}, u32[]{:S(2)}, u32[]{:S(2)}) %all-to-all-start.1) | async-done | bytes 262176 | tf_op jit(solution)/shard_map/all_to_all | solution.py:45
  61.1 6.4 %scatter_custom_fusion = bf16[2048,32]{1,0:T(8,128)(2,1)S(1)} fusion(s32[1024]{0:T(1024)S(1)} %bitcast.74, bf16[512,32]{1,0:T(8,128)(2,1)S(1)} %copy.79, s32[1024]{0:T(1024)S(1)} %broadcast_clamp_fusion.1, bf16[]{:T(256)} %constant.18.clone.1), kind=kCustom, calls=%fused_computation.22 | custom fusion | bytes 131074 | tf_op jit(solution)/shard_map/scatter | solution.py:59
  67.7 20.9 %all_to_all.28 = bf16[8,256,32]{1,2,0:T(8,128)(2,1)} all-to-all(bf16[8,256,32]{1,2,0:T(8,128)(2,1)S(1)} %copy.81), channel_id=1, replica_groups=mesh['ey'=1,'ec'=8,'mx'=4,'mzh'=2,'mzl'=8] {'mx','mzh'}, dimensions={0} | all-to-all | bytes 262144 | tf_op jit(solution)/shard_map/all_to_all | solution.py:61
  88.8 1.2 pad_maximum_fusion
  90.0 62.6 %all-gather.10.cloned.1.call-done = bf16[64,256,32]{1,2,0:T(8,128)(2,1)} async-done(((bf16[8,256,32]{1,2,0:T(8,128)(2,1)}), bf16[64,256,32]{1,2,0:T(8,128)(2,1)}) %all-gather.10.cloned.1.call-update) | async-done | bytes 1048592 | tf_op jit(solution)/shard_map/all_gather | solution.py:69
  152.6 1.3 copy.82
  153.9 64.0 %all-gather.8.cloned.1.call-done = bf16[3,704,2048]{2,1,0:T(8,128)(2,1)} async-done(((bf16[3,704,256]{2,1,0:T(8,128)(2,1)}), bf16[3,704,2048]{2,1,0:T(8,128)(2,1)}) %all-gather.8.cloned.1.call-update) | async-done | bytes 8650768 | tf_op jit(solution)/shard_map/all_gather | solution.py:73
  217.9 2.7 fusion.2
  220.6 6.0 %fusion.3 = bf16[256,2048]{1,0:T(8,128)(2,1)S(1)} fusion(bf16[3,704,2048]{2,1,0:T(8,128)(2,1)} %all-gather.8.cloned.1.call-done, bf16[256,2048]{0,1:T(8,128)(2,1)S(1)} %bitcast.68, f32[256,704]{0,1:T(8,128)S(1)} %fusion.2), kind=kOutput, calls=%fused_computation.10 | convolution fusion | flops 1478000640 | bytes 8585216 | tf_op jit(solution)/shard_map/dot_general | solution.py:77
  226.6 1.3 copy.83
  227.9 15.5 %all-to-all-start.3 = ((bf16[256,64,32]{0,2,1:T(8,128)(2,1)}), bf16[256,64,32]{0,2,1:T(8,128)(2,1)S(1)}, u32[]{:S(2)}, u32[]{:S(2)}) async-start(bf16[256,64,32]{0,2,1:T(8,128)(2,1)} %bitcast.17), calls=%async_computation.3 | async-start | bytes 2097152 | tf_op jit(solution)/shard_map/all_to_all | solution.py:78
  243.8 50.3 %all-to-all-done.3 = bf16[256,64,32]{0,2,1:T(8,128)(2,1)S(1)} async-done(((bf16[256,64,32]{0,2,1:T(8,128)(2,1)}), bf16[256,64,32]{0,2,1:T(8,128)(2,1)S(1)}, u32[]{:S(2)}, u32[]{:S(2)}) %all-to-all-start.3) | async-done | bytes 1048608 | tf_op jit(solution)/shard_map/all_to_all | solution.py:78
  294.6 2.8 gather_fusion
  297.4 2.8 multiply_reduce_fusion
  300.4 22.4 %all-gather.3 = f32[16,1,512]{2,1,0:T(1,128)S(1)} all-gather(f32[1,1,512]{2,1,0:T(1,128)S(1)} %bitcast.79), channel_id=3, replica_groups=mesh['ey'=1,'ec'=8,'mx'=4,'mzh'=2,'mzl'=8] {'mzh','mzl'}, dimensions={0}, use_global_device_ids=true | all-gather | bytes 34816 | tf_op jit(solution)/shard_map/all_gather | solution.py:88
  322.8 9.5 %all-gather.4 = f32[4,1,512]{2,1,0:T(1,128)S(1)} all-gather(f32[1,1,512]{2,1,0:T(1,128)S(1)} %bitcast.78), channel_id=4, replica_groups=mesh['ey'=1,'ec'=8,'mx'=4,'mzh'=2,'mzl'=8] {'mx'}, dimensions={0}, use_global_device_ids=true | all-gather | bytes 10240 | tf_op jit(solution)/shard_map/all_gather | solution.py:89
  332.5 23.2 %all_gather.35 = bf16[4096,32]{0,1:T(8,128)(2,1)S(1)} all-gather(bf16[512,32]{0,1:T(8,128)(2,1)S(1)} %multiply_convert_fusion), channel_id=1, replica_groups=mesh['ey'=1,'ec'=8,'mx'=4,'mzh'=2,'mzl'=8] {'ey','ec'}, dimensions={0}, use_global_device_ids=true | all-gather | bytes 294912 | tf_op jit(solution)/shard_map/all_gather | solution.py:93
  356.2 1.3 gather_fusion.1
  (54 shorter events, 5.8 us)
Async XLA Ops:
  6.5 12.0 %copy-start.3 = (bf16[512,32]{0,1:T(8,128)(2,1)S(1)}, bf16[512,32]{0,1:T(8,128)(2,1)}, u32[]{:S(2)}) copy-start(bf16[512,32]{0,1:T(8,128)(2,1)} %param.9) | copy-start | bytes 98308
  8.3 42.2 %all-to-all-start = ((bf16[4,32,2048]{2,1,0:T(8,128)(2,1)}), bf16[4,32,2048]{2,1,0:T(8,128)(2,1)S(1)}, u32[]{:S(2)}, u32[]{:S(2)}) async-start(bf16[4,32,2048]{2,1,0:T(8,128)(2,1)} %broadcast_in_dim.8), calls=%async_computation | async-start | bytes 1048576 | tf_op jit(solution)/shard_map/all_to_all | solution.py:35
  14.1 74.6 %copy-start = (bf16[704,256]{1,0:T(8,128)(2,1)S(1)}, bf16[704,256]{1,0:T(8,128)(2,1)}, u32[]{:S(2)}) copy-start(bf16[704,256]{1,0:T(8,128)(2,1)} %param.15) | copy-start | bytes 1081348
  14.1 74.6 %copy-start.1 = (bf16[704,256]{1,0:T(8,128)(2,1)S(1)}, bf16[704,256]{1,0:T(8,128)(2,1)}, u32[]{:S(2)}) copy-start(bf16[704,256]{1,0:T(8,128)(2,1)} %param.14) | copy-start | bytes 1081348
  14.2 74.6 %copy-start.2 = (bf16[704,256]{1,0:T(8,128)(2,1)S(1)}, bf16[704,256]{1,0:T(8,128)(2,1)}, u32[]{:S(2)}) copy-start(bf16[704,256]{1,0:T(8,128)(2,1)} %param.13) | copy-start | bytes 1081348
  51.4 9.6 %all-to-all-start.1 = ((f32[512,4,32]{0,2,1:T(8,128)}), f32[512,4,32]{0,2,1:T(8,128)S(1)}, u32[]{:S(2)}, u32[]{:S(2)}) async-start(f32[512,4,32]{0,2,1:T(8,128)} %bitcast.2), calls=%async_computation.1 | async-start | bytes 524288 | tf_op jit(solution)/shard_map/all_to_all | solution.py:45
  55.4 97.1 %all-gather.10.cloned.1.call-start = ((), (), s32[]{:S(2)}) async-start(), calls=%async_computation.5 | async-start | bytes 1179648 | tf_op jit(solution)/shard_map/all_gather | solution.py:69
  88.7 129.2 %all-gather.8.cloned.1.call-start = ((), (), s32[]{:S(2)}) async-start(), calls=%async_computation.4 | async-start | bytes 9732096 | tf_op jit(solution)/shard_map/all_gather | solution.py:73
  226.6 16.9 %copy-start.4 = (f32[512,2]{0,1:T(2,128)S(1)}, f32[512,2]{0,1:T(2,128)}, u32[]{:S(2)}) copy-start(f32[512,2]{0,1:T(2,128)} %param.12) | copy-start | bytes 12292
  226.6 17.2 %copy-start.5 = (s32[512]{0:T(512)S(1)}, s32[512]{0:T(512)}, u32[]{:S(2)}) copy-start(s32[512]{0:T(512)} %param.17) | copy-start | bytes 6148
  227.9 66.2 %all-to-all-start.3 = ((bf16[256,64,32]{0,2,1:T(8,128)(2,1)}), bf16[256,64,32]{0,2,1:T(8,128)(2,1)S(1)}, u32[]{:S(2)}, u32[]{:S(2)}) async-start(bf16[256,64,32]{0,2,1:T(8,128)(2,1)} %bitcast.17), calls=%async_computation.3 | async-start | bytes 2097152 | tf_op jit(solution)/shard_map/all_to_all | solution.py:78
  294.6 37.8 %copy-start.6 = (f32[32]{0:T(128)S(1)}, f32[32]{0:T(128)}, u32[]{:S(2)}) copy-start(f32[32]{0:T(128)} %param.16) | copy-start | bytes 388
Sparse Core Ops, SparseCore 0:
  88.8 63.6 all-gather.9
  154.7 63.1 all-gather.7
where the time goes:
time: 366 us; the launch traced here: 365 us
  waiting for transfers between devices  182 us (50%)
  blocking collectives  108 us (30%)
  starting transfers between devices  24.5 us (7%)
  local copies, waits for them, and re-layouts  19.2 us (5%)
  between operations  13.7 us (4%)
  matrix products  9.63 us (3%)
  other arithmetic  7.73 us (2%)
    all_gather x1, waiting for transfers between devices, shards(): lax.all_gather(jnp.stack([w_gate, w_up, w_down]), EX, axis=2, tiled=True)  64 us
    all_gather x1, waiting for transfers between devices, shards(): lax.all_gather(one_copy, 'mzl', axis=0).transpose(2, 1, 0, 3)  62.6 us
    all_to_all x1, waiting for transfers between devices, shards(): lax.all_to_all(partial_value.astype(jnp.bfloat16), MP, split_axis=1, conc...  50.3 us
    all_gather x1, blocking collectives, shards(): along_z = lax.all_gather(context, MZ, axis=1, tiled=True)  31.9 us
    all_gather x1, blocking collectives, shards(): everyone = lax.all_gather(normed, EX, axis=0, tiled=True)  23.2 us
    all_gather x1, blocking collectives, shards(): lax.all_gather(jnp.sum(combined * combined, axis=1), MZ, axis=0)  22.4 us
    all_to_all x1, blocking collectives, shards(): lax.all_to_all(slotted.reshape(EXPERTS, capacity, feat_local), ('mx', 'mz...  20.9 us
    all_to_all x1, starting transfers between devices, shards(): lax.all_to_all(partial_value.astype(jnp.bfloat16), MP, split_axis=1, conc...  15.5 us
  transfers between devices with their start and end apart: 5, of which 4 were waited for; matrix products, arithmetic and copies ran while one was open for 2% of the time, Pallas kernels for 0%

commit v1 on v0

--- a/solution.py
+++ b/solution.py
@@ -70,7 +70,12 @@
         .transpose(2, 1, 0, 3)
         .reshape(capacity, mp_count * feat_local)
     )
-    stacked = lax.all_gather(jnp.stack([w_gate, w_up, w_down]), EX, axis=2, tiled=True)
+    stacked = jnp.concatenate(
+        lax.all_to_all(
+            jnp.stack([jnp.stack([w_gate, w_up, w_down])] * lax.axis_size(EX)), EX, 0, 0
+        ),
+        axis=2,
+    )
     gate_next = jnp.einsum("rd,hd->rh", inbox_rows, stacked[0], preferred_element_type=jnp.float32)
     up_next = jnp.einsum("rd,hd->rh", inbox_rows, stacked[1], preferred_element_type=jnp.float32)
     activated = (jax.nn.silu(gate_next) * up_next).astype(jnp.bfloat16)

time: 366 us -> 353 us (0.964)
  blocking collectives: 108 us -> 87.2 us
  waiting for transfers between devices: 182 us -> 164 us
  local copies, waits for them, and re-layouts: 19.2 us -> 33.6 us
  starting transfers between devices: 24.5 us -> 37.9 us
    all_gather x1 -> x0, waiting for transfers between devices: 64 us -> none  [shards(): lax.all_gather(jnp.stack([w_gate, w_up, w_down]), EX, axis=2, tiled=True)]
    all_to_all x0 -> x2, waiting for transfers between devices: none -> 52.7 us  [the longest x1 38.6 us: shards(): lax.all_to_all(jnp.stack([jnp.stack([w_gate, w_up, w_down])] * lax.axis_s...]
    all_to_all x0 -> x2, starting transfers between devices: none -> 22.8 us  [the longest x1 16 us: shards(): lax.all_to_all(jnp.stack([jnp.stack([w_gate, w_up, w_down])] * lax.axis_s...]
    all_to_all x1 -> x0, blocking collectives: 20.9 us -> none  [shards(): lax.all_to_all(slotted.reshape(EXPERTS, capacity, feat_local), ('mx', 'mz...]
    all_to_all x1, starting transfers between devices: 15.5 us -> 6.03 us  [shards(): lax.all_to_all(partial_value.astype(jnp.bfloat16), MP, split_axis=1, conc...]
    all_gather x1, waiting for transfers between devices: 62.6 us -> 55.1 us  [shards(): lax.all_gather(one_copy, 'mzl', axis=0).transpose(2, 1, 0, 3)]
    another operation x0 -> x1, local copies, waits for them, and re-layouts: none -> 4.24 us  [shards(): jnp.stack([jnp.stack([w_gate, w_up, w_down])] * lax.axis_size(EX))]
    slice x1 -> x2, local copies, waits for them, and re-layouts: 0.28 us -> 4.29 us  [the longest x1 4.01 us: shards(): stacked[0]]
  transfers between devices with their start and end apart: 5 -> 6, of which waited for: 4 -> 5; matrix products, arithmetic and copies ran while one was open for 2% -> 2% of each run, Pallas kernels for 0% -> 0%
where the time goes in v1:
time: 353 us; the launch traced here: 352 us
  waiting for transfers between devices  164 us (46%)
  blocking collectives  87.2 us (25%)
  starting transfers between devices  37.9 us (11%)
  local copies, waits for them, and re-layouts  33.6 us (10%)
  between operations  13.7 us (4%)
  matrix products  9.22 us (3%)
  other arithmetic  6.57 us (2%)
    all_gather x1, waiting for transfers between devices, shards(): lax.all_gather(one_copy, 'mzl', axis=0).transpose(2, 1, 0, 3)  55.1 us
    all_to_all x1, waiting for transfers between devices, shards(): lax.all_to_all(partial_value.astype(jnp.bfloat16), MP, split_axis=1, conc...  49.9 us
    all_to_all x1, waiting for transfers between devices, shards(): lax.all_to_all(jnp.stack([jnp.stack([w_gate, w_up, w_down])] * lax.axis_s...  38.6 us
    all_gather x1, blocking collectives, shards(): along_z = lax.all_gather(context, MZ, axis=1, tiled=True)  31.7 us
    all_gather x1, blocking collectives, shards(): everyone = lax.all_gather(normed, EX, axis=0, tiled=True)  24.6 us
    all_gather x1, blocking collectives, shards(): lax.all_gather(jnp.sum(combined * combined, axis=1), MZ, axis=0)  22.5 us
    all_to_all x1, starting transfers between devices, shards(): lax.all_to_all(jnp.stack([jnp.stack([w_gate, w_up, w_down])] * lax.axis_s...  16 us
    all_to_all x1, waiting for transfers between devices, shards(): lax.all_to_all(slotted.reshape(EXPERTS, capacity, feat_local), ('mx', 'mz...  14.1 us
  transfers between devices with their start and end apart: 6, of which 5 were waited for; matrix products, arithmetic and copies ran while one was open for 2% of the time, Pallas kernels for 0%

profile of v1, /device:TPU:1, one launch (start us, length us, event | category | flops | bytes accessed | tf_op | source)
XLA Modules:
  0.0 352.0 jit_solution(13428595350731919591)
XLA Ops:
  8.3 4.8 %all-to-all-start = ((bf16[4,32,2048]{2,1,0:T(8,128)(2,1)}), bf16[4,32,2048]{2,1,0:T(8,128)(2,1)S(1)}, u32[]{:S(2)}, u32[]{:S(2)}) async-start(bf16[4,32,2048]{2,1,0:T(8,128)(2,1)} %broadcast_in_dim.8), calls=%async_computation | async-start | bytes 1048576 | tf_op jit(solution)/shard_map/all_to_all | solution.py:35
  15.4 2.3 reduce-window.6
  18.4 31.7 %all_gather.24 = bf16[512,512]{0,1:T(8,128)(2,1)S(1)} all-gather(bf16[512,32]{0,1:T(8,128)(2,1)S(1)} %copy-done.5), channel_id=1, replica_groups=mesh['ey'=1,'ec'=8,'mx'=4,'mzh'=2,'mzl'=8] {'mzh','mzl'}, dimensions={1}, use_global_device_ids=true | all-gather | bytes 557056 | tf_op jit(solution)/shard_map/all_gather | solution.py:33
  51.1 4.2 %all-to-all-start.1 = ((f32[512,4,32]{0,2,1:T(8,128)}), f32[512,4,32]{0,2,1:T(8,128)S(1)}, u32[]{:S(2)}, u32[]{:S(2)}) async-start(f32[512,4,32]{0,2,1:T(8,128)} %bitcast.2), calls=%async_computation.1 | async-start | bytes 524288 | tf_op jit(solution)/shard_map/all_to_all | solution.py:45
  55.4 5.5 %all-to-all-done.1 = f32[512,4,32]{0,2,1:T(8,128)S(1)} async-done(((f32[512,4,32]{0,2,1:T(8,128)}), f32[512,4,32]{0,2,1:T(8,128)S(1)}, u32[]{:S(2)}, u32[]{:S(2)}) %all-to-all-start.1) | async-done | bytes 262176 | tf_op jit(solution)/shard_map/all_to_all | solution.py:45
  61.0 6.4 %scatter_custom_fusion = bf16[2048,32]{1,0:T(8,128)(2,1)S(1)} fusion(s32[1024]{0:T(1024)S(1)} %bitcast.79, bf16[512,32]{1,0:T(8,128)(2,1)S(1)} %copy.88, s32[1024]{0:T(1024)S(1)} %broadcast_clamp_fusion.1, bf16[]{:T(256)} %constant.18.clone.1), kind=kCustom, calls=%fused_computation.11 | custom fusion | bytes 131074 | tf_op jit(solution)/shard_map/scatter | solution.py:59
  68.3 6.8 %all-to-all-start.2 = ((bf16[8,256,32]{1,2,0:T(8,128)(2,1)}), bf16[8,256,32]{1,2,0:T(8,128)(2,1)S(1)}, u32[]{:S(2)}, u32[]{:S(2)}) async-start(bf16[8,256,32]{1,2,0:T(8,128)(2,1)} %copy.90), calls=%async_computation.2 | async-start | bytes 262144 | tf_op jit(solution)/shard_map/all_to_all | solution.py:61
  75.2 14.1 %all-to-all-done.2 = bf16[8,256,32]{1,2,0:T(8,128)(2,1)S(1)} async-done(((bf16[8,256,32]{1,2,0:T(8,128)(2,1)}), bf16[8,256,32]{1,2,0:T(8,128)(2,1)S(1)}, u32[]{:S(2)}, u32[]{:S(2)}) %all-to-all-start.2) | async-done | bytes 131104 | tf_op jit(solution)/shard_map/all_to_all | solution.py:61
  89.3 4.2 %stack.27 = bf16[8,3,704,256]{3,2,1,0:T(8,128)(2,1)} broadcast(bf16[3,704,256]{2,1,0:T(8,128)(2,1)S(1)} %pad_maximum_fusion), dimensions={1,2,3} | broadcast | bytes 9732096 | tf_op jit(solution)/shard_map/stack | solution.py:75
  93.6 16.0 %all-to-all-start.3 = ((bf16[8,3,704,256]{3,2,1,0:T(8,128)(2,1)}), bf16[8,3,704,256]{3,2,1,0:T(8,128)(2,1)}, u32[]{:S(2)}, u32[]{:S(2)}) async-start(bf16[8,3,704,256]{3,2,1,0:T(8,128)(2,1)} %stack.27), calls=%async_computation.3 | async-start | bytes 17301504 | tf_op jit(solution)/shard_map/all_to_all | solution.py:74
  110.3 55.1 %all-gather.7.cloned.1.call-done = bf16[64,256,32]{1,2,0:T(8,128)(2,1)} async-done(((bf16[8,256,32]{1,2,0:T(8,128)(2,1)}), bf16[64,256,32]{1,2,0:T(8,128)(2,1)}) %all-gather.7.cloned.1.call-update) | async-done | bytes 1048592 | tf_op jit(solution)/shard_map/all_gather | solution.py:69
  165.4 2.3 copy.91
  167.7 38.6 %all-to-all-done.3 = bf16[8,3,704,256]{3,2,1,0:T(8,128)(2,1)} async-done(((bf16[8,3,704,256]{3,2,1,0:T(8,128)(2,1)}), bf16[8,3,704,256]{3,2,1,0:T(8,128)(2,1)}, u32[]{:S(2)}, u32[]{:S(2)}) %all-to-all-start.3) | async-done | bytes 8650784 | tf_op jit(solution)/shard_map/all_to_all | solution.py:74
  206.3 4.0 %fusion.13 = (bf16[1,704,8,256]{3,1,0,2:T(8,128)(2,1)S(1)}, bf16[1,704,8,256]{3,1,0,2:T(8,128)(2,1)S(1)}, bf16[1,704,8,256]{3,1,0,2:T(8,128)(2,1)S(1)}) fusion(bf16[3,704,8,256]{3,1,0,2:T(8,128)(2,1)} %bitcast.14), kind=kLoop, calls=%fused_computation.39 | loop fusion | bytes 17301504 | tf_op jit(solution)/shard_map/slice | solution.py:79
  210.7 2.0 copy.105
  215.7 6.5 %convolution_convert_fusion = bf16[256,2048]{1,0:T(8,128)(2,1)} fusion(bf16[704,2048]{1,0:T(8,128)(2,1)S(1)} %bitcast.66, bf16[704,2048]{1,0:T(8,128)(2,1)} %bitcast.67, bf16[256,2048]{0,1:T(8,128)(2,1)} %bitcast.71, f32[256,704]{0,1:T(8,128)} %fusion.14), kind=kOutput, calls=%fused_computation.4 | convolution fusion | flops 1478000640 | bytes 8585216 | tf_op jit(solution)/shard_map/dot_general | solution.py:82
  222.2 2.3 copy.95
  224.5 6.0 %all-to-all-start.4 = ((bf16[256,64,32]{0,2,1:T(8,128)(2,1)}), bf16[256,64,32]{0,2,1:T(8,128)(2,1)S(1)}, u32[]{:S(2)}, u32[]{:S(2)}) async-start(bf16[256,64,32]{0,2,1:T(8,128)(2,1)} %bitcast.15), calls=%async_computation.4 | async-start | bytes 2097152 | tf_op jit(solution)/shard_map/all_to_all | solution.py:83
  230.9 49.9 %all-to-all-done.4 = bf16[256,64,32]{0,2,1:T(8,128)(2,1)S(1)} async-done(((bf16[256,64,32]{0,2,1:T(8,128)(2,1)}), bf16[256,64,32]{0,2,1:T(8,128)(2,1)S(1)}, u32[]{:S(2)}, u32[]{:S(2)}) %all-to-all-start.4) | async-done | bytes 1048608 | tf_op jit(solution)/shard_map/all_to_all | solution.py:83
  281.3 2.8 gather_fusion
  284.1 2.8 multiply_reduce_fusion
  287.0 22.5 %all-gather.3 = f32[16,1,512]{2,1,0:T(1,128)S(1)} all-gather(f32[1,1,512]{2,1,0:T(1,128)S(1)} %bitcast.84), channel_id=3, replica_groups=mesh['ey'=1,'ec'=8,'mx'=4,'mzh'=2,'mzl'=8] {'mzh','mzl'}, dimensions={0}, use_global_device_ids=true | all-gather | bytes 34816 | tf_op jit(solution)/shard_map/all_gather | solution.py:93
  309.6 8.4 %all-gather.4 = f32[4,1,512]{2,1,0:T(1,128)S(1)} all-gather(f32[1,1,512]{2,1,0:T(1,128)S(1)} %bitcast.83), channel_id=4, replica_groups=mesh['ey'=1,'ec'=8,'mx'=4,'mzh'=2,'mzl'=8] {'mx'}, dimensions={0}, use_global_device_ids=true | all-gather | bytes 10240 | tf_op jit(solution)/shard_map/all_gather | solution.py:94
  318.1 24.6 %all_gather.31 = bf16[4096,32]{0,1:T(8,128)(2,1)S(1)} all-gather(bf16[512,32]{0,1:T(8,128)(2,1)S(1)} %multiply_convert_fusion), channel_id=1, replica_groups=mesh['ey'=1,'ec'=8,'mx'=4,'mzh'=2,'mzl'=8] {'ey','ec'}, dimensions={0}, use_global_device_ids=true | all-gather | bytes 294912 | tf_op jit(solution)/shard_map/all_gather | solution.py:98
  (63 shorter events, 14.4 us)
Async XLA Ops:
  6.5 11.9 %copy-start.5 = (bf16[512,32]{0,1:T(8,128)(2,1)S(1)}, bf16[512,32]{0,1:T(8,128)(2,1)}, u32[]{:S(2)}) copy-start(bf16[512,32]{0,1:T(8,128)(2,1)} %param.9) | copy-start | bytes 98308
  8.3 41.9 %all-to-all-start = ((bf16[4,32,2048]{2,1,0:T(8,128)(2,1)}), bf16[4,32,2048]{2,1,0:T(8,128)(2,1)S(1)}, u32[]{:S(2)}, u32[]{:S(2)}) async-start(bf16[4,32,2048]{2,1,0:T(8,128)(2,1)} %broadcast_in_dim.8), calls=%async_computation | async-start | bytes 1048576 | tf_op jit(solution)/shard_map/all_to_all | solution.py:35
  14.7 60.4 %copy-start.2 = (bf16[704,256]{1,0:T(8,128)(2,1)S(1)}, bf16[704,256]{1,0:T(8,128)(2,1)}, u32[]{:S(2)}) copy-start(bf16[704,256]{1,0:T(8,128)(2,1)} %param.15) | copy-start | bytes 1081348
  14.7 60.4 %copy-start.3 = (bf16[704,256]{1,0:T(8,128)(2,1)S(1)}, bf16[704,256]{1,0:T(8,128)(2,1)}, u32[]{:S(2)}) copy-start(bf16[704,256]{1,0:T(8,128)(2,1)} %param.14) | copy-start | bytes 1081348
  14.7 60.4 %copy-start.4 = (bf16[704,256]{1,0:T(8,128)(2,1)S(1)}, bf16[704,256]{1,0:T(8,128)(2,1)}, u32[]{:S(2)}) copy-start(bf16[704,256]{1,0:T(8,128)(2,1)} %param.13) | copy-start | bytes 1081348
  51.1 9.8 %all-to-all-start.1 = ((f32[512,4,32]{0,2,1:T(8,128)}), f32[512,4,32]{0,2,1:T(8,128)S(1)}, u32[]{:S(2)}, u32[]{:S(2)}) async-start(f32[512,4,32]{0,2,1:T(8,128)} %bitcast.2), calls=%async_computation.1 | async-start | bytes 524288 | tf_op jit(solution)/shard_map/all_to_all | solution.py:45
  68.3 21.0 %all-to-all-start.2 = ((bf16[8,256,32]{1,2,0:T(8,128)(2,1)}), bf16[8,256,32]{1,2,0:T(8,128)(2,1)S(1)}, u32[]{:S(2)}, u32[]{:S(2)}) async-start(bf16[8,256,32]{1,2,0:T(8,128)(2,1)} %copy.90), calls=%async_computation.2 | async-start | bytes 262144 | tf_op jit(solution)/shard_map/all_to_all | solution.py:61
  89.3 4.2 %copy-start.1 = (bf16[8,256,32]{1,2,0:T(8,128)(2,1)}, bf16[8,256,32]{1,2,0:T(8,128)(2,1)S(1)}, u32[]{:S(2)}) copy-start(bf16[8,256,32]{1,2,0:T(8,128)(2,1)S(1)} %all-to-all-done.2) | copy-start | bytes 393220
  93.6 112.7 %all-to-all-start.3 = ((bf16[8,3,704,256]{3,2,1,0:T(8,128)(2,1)}), bf16[8,3,704,256]{3,2,1,0:T(8,128)(2,1)}, u32[]{:S(2)}, u32[]{:S(2)}) async-start(bf16[8,3,704,256]{3,2,1,0:T(8,128)(2,1)} %stack.27), calls=%async_computation.3 | async-start | bytes 17301504 | tf_op jit(solution)/shard_map/all_to_all | solution.py:74
  109.6 55.8 %all-gather.7.cloned.1.call-start = ((), (), s32[]{:S(2)}) async-start(), calls=%async_computation.5 | async-start | bytes 1179648 | tf_op jit(solution)/shard_map/all_gather | solution.py:69
  212.7 1.2 copy-start
  222.2 8.3 %copy-start.6 = (f32[512,2]{0,1:T(2,128)S(1)}, f32[512,2]{0,1:T(2,128)}, u32[]{:S(2)}) copy-start(f32[512,2]{0,1:T(2,128)} %param.12) | copy-start | bytes 12292
  222.2 8.7 %copy-start.7 = (s32[512]{0:T(512)S(1)}, s32[512]{0:T(512)}, u32[]{:S(2)}) copy-start(s32[512]{0:T(512)} %param.17) | copy-start | bytes 6148
  224.5 56.3 %all-to-all-start.4 = ((bf16[256,64,32]{0,2,1:T(8,128)(2,1)}), bf16[256,64,32]{0,2,1:T(8,128)(2,1)S(1)}, u32[]{:S(2)}, u32[]{:S(2)}) async-start(bf16[256,64,32]{0,2,1:T(8,128)(2,1)} %bitcast.15), calls=%async_computation.4 | async-start | bytes 2097152 | tf_op jit(solution)/shard_map/all_to_all | solution.py:83
  281.3 36.8 %copy-start.8 = (f32[32]{0:T(128)S(1)}, f32[32]{0:T(128)}, u32[]{:S(2)}) copy-start(f32[32]{0:T(128)} %param.16) | copy-start | bytes 388
Sparse Core Ops, SparseCore 0:
  112.5 52.8 all-gather.6
